TPU v7x, 256 devices: a whole 4x4x8 slice. The times are simulated.
256 devices in a mesh: dp: 16 (over y, x), expert: 16 (over z, core).
Axes of the slice: x: 4, y: 4, z: 8, core: 2. Of those that a mesh axis runs over, the one named last changes fastest.
Arguments:
- tokens: bfloat16 [32768, 768], P(('dp', 'expert')), may hold values from -6 to 6
- cotangent: bfloat16 [32768, 768], P(('dp', 'expert')), may hold values from -6 to 6
- routes: int32 [32768, 2], P(('dp', 'expert')), may hold values from 0 to 15, all different within a row; in each aligned block of 128 rows (0 to 127, 128 to 255, ...) at most 48 rows name the same one
- gates: float32 [32768, 2], P(('dp', 'expert')), may hold values from 0.1 to 1
- w_in: bfloat16 [16, 2304, 768], P('expert', 'dp'), may hold values from -0.21875 to 0.21875
- w_out: bfloat16 [16, 2304, 768], P('expert', 'dp'), may hold values from -0.125 to 0.125
Outputs:
- d_tokens: bfloat16 [32768, 768], P(('dp', 'expert'))
- grad_in: float32 [16, 2304, 768], P('expert', 'dp')
- grad_out: float32 [16, 2304, 768], P('expert', 'dp')
Inputs may be any that keep to these rules, and one draw needn't show every extreme that they name: `routes`: within the rows of one device (128 rows) no expert is named more than 48 times, and in every draw some expert is named exactly 48 times by the rows of some device; the 2 entries of a row differ.
All inputs are finite; a program needn't handle non-finite values.
Results may differ from a plain program's by a relative error of at most 0.015.
Values may be sent and summed in bfloat16 or wider, within the bound.
No kernel may reach another device: no remote copies, remote signals or barrier semaphores. Data moves between devices by JAX's collectives and lax.ppermute only.
A program may use at most 64 MiB of HBM per device.

v0:
```python
import jax
import jax.numpy as jnp
from jax import lax
from jax.sharding import PartitionSpec as P

tanh_coef = 0.7978845608028654
cubic_coef = 0.044715


def gelu_tanh(value):
    inner = tanh_coef * (value + cubic_coef * value * value * value)
    return 0.5 * value * (1.0 + jnp.tanh(inner))


def gelu_slope(value):
    inner = tanh_coef * (value + cubic_coef * value * value * value)
    slope_t = jnp.tanh(inner)
    return 0.5 * (1.0 + slope_t) + 0.5 * value * (1.0 - slope_t * slope_t) * tanh_coef * (
        1.0 + 3.0 * cubic_coef * value * value
    )


def dispatch_tables(route_blk, gate_blk, experts, capacity):
    tok_rows = route_blk.shape[0]
    flat = route_blk.reshape(-1)
    onehot = (flat[:, None] == jnp.arange(experts, dtype=jnp.int32)[None, :]).astype(jnp.int32)
    before = jnp.cumsum(onehot, axis=0) - onehot
    position = jnp.sum(before * onehot, axis=1)
    slots = (flat * capacity + position).reshape(tok_rows, -1)
    slot_ids = jnp.arange(experts * capacity, dtype=jnp.int32)
    placed = slot_ids[:, None, None] == slots[None, :, :]
    route_mat = jnp.sum(placed.astype(jnp.int32), axis=2).astype(jnp.bfloat16)
    gate_slot = jnp.sum(jnp.where(placed, gate_blk[None, :, :], jnp.float32(0.0)), axis=(1, 2))
    return (route_mat, gate_slot)


def shards(tokens, cotangent, routes, gates, w_in, w_out):
    experts = lax.axis_size("expert")
    tok_rows, model_width = tokens.shape
    top_count = routes.shape[1]
    capacity = 3 * tok_rows * top_count // experts
    shard_rows = w_in.shape[1]
    slot_rows = experts * capacity
    route_mat, gate_slot = dispatch_tables(routes, gates, experts, capacity)
    rows_sent = jnp.dot(route_mat, tokens, preferred_element_type=jnp.float32).astype(jnp.bfloat16)
    grad_rows = jnp.dot(route_mat, cotangent, preferred_element_type=jnp.float32)
    grads_sent = (gate_slot[:, None] * grad_rows).astype(jnp.bfloat16)
    rows_recv, grads_recv = (
        lax.all_to_all(
            rows_sent.reshape(experts, capacity, model_width),
            "expert",
            split_axis=0,
            concat_axis=0,
            tiled=True,
        ),
        lax.all_to_all(
            grads_sent.reshape(experts, capacity, model_width),
            "expert",
            split_axis=0,
            concat_axis=0,
            tiled=True,
        ),
    )
    rows_in = rows_recv.reshape(slot_rows, model_width)
    grads_in = grads_recv.reshape(slot_rows, model_width)
    piece_in = lax.all_gather(w_in[0], "dp", axis=0, tiled=True)
    piece_out = lax.all_gather(w_out[0], "dp", axis=0, tiled=True)
    pre = lax.dot_general(
        rows_in, piece_in, (((1,), (1,)), ((), ())), preferred_element_type=jnp.float32
    )
    acts = gelu_tanh(pre).astype(jnp.bfloat16)
    grad_act = lax.dot_general(
        grads_in, piece_out, (((1,), (1,)), ((), ())), preferred_element_type=jnp.float32
    )
    dpre = (grad_act * gelu_slope(pre)).astype(jnp.bfloat16)
    slot_sum = jnp.dot(dpre, piece_in, preferred_element_type=jnp.float32)
    slot_sum, acts_all, dpre_all = (slot_sum, acts, dpre)
    returned = lax.all_to_all(
        slot_sum.astype(jnp.bfloat16).reshape(experts, capacity, model_width),
        "expert",
        split_axis=0,
        concat_axis=0,
        tiled=True,
    )
    token_grads = lax.dot_general(
        route_mat,
        returned.reshape(slot_rows, model_width),
        (((0,), (0,)), ((), ())),
        preferred_element_type=jnp.float32,
    )
    d_tokens = token_grads.astype(jnp.bfloat16)
    term_in = lax.dot_general(
        dpre_all, rows_in, (((0,), (0,)), ((), ())), preferred_element_type=jnp.float32
    )
    term_out = lax.dot_general(
        acts_all, grads_in, (((0,), (0,)), ((), ())), preferred_element_type=jnp.float32
    )
    summed = lax.psum(
        jnp.concatenate([term_in, term_out], axis=1).astype(jnp.bfloat16), "dp"
    ).astype(jnp.float32)
    own_rows = lax.dynamic_slice_in_dim(summed, lax.axis_index("dp") * shard_rows, shard_rows, 0)
    grad_in = own_rows[:, :model_width][None]
    grad_out = own_rows[:, model_width:][None]
    return (d_tokens, grad_in, grad_out)


def solution(mesh):
    in_specs = (
        P(("dp", "expert"), None),
        P(("dp", "expert"), None),
        P(("dp", "expert"), None),
        P(("dp", "expert"), None),
        P("expert", "dp", None),
        P("expert", "dp", None),
    )
    out_specs = (P(("dp", "expert"), None), P("expert", "dp", None), P("expert", "dp", None))
    return jax.shard_map(shards, mesh=mesh, in_specs=in_specs, out_specs=out_specs, check_vma=False)
```

profile of v0, /device:TPU:1, one launch (start us, length us, event | category | flops | bytes accessed | tf_op | source)
XLA Modules:
  0.0 294.6 jit_solution(5425610005325512928)
XLA Ops:
  7.2 0.7 all-gather.7.cloned.1.call-update
  8.0 0.7 all-gather.5.cloned.1.call-update
  8.7 0.8 copy.29
  9.6 0.1 eq.43
  9.8 0.6 reduce-window.6
  10.4 0.2 slice_reduce_fusion
  10.7 0.1 reduce_sum.30
  10.9 0.7 multiply_add_fusion.1
  11.7 1.5 convolution_convert_fusion.2
  13.2 10.0 %all-to-all-start.1 = ((bf16[16,48,768]{2,1,0:T(8,128)(2,1)}), bf16[16,48,768]{2,1,0:T(8,128)(2,1)S(1)}, u32[]{:S(2)}, u32[]{:S(2)}) async-start(bf16[16,48,768]{2,1,0:T(8,128)(2,1)} %bitcast.4), calls=%async_computation.1 | async-start | bytes 2359296 | tf_op jit(solution)/shard_map/all_to_all | solution.py:49
  23.2 0.2 select_reduce_fusion
  23.4 1.5 multiply_convert_fusion.2
  24.9 28.9 %all-to-all-done.1 = bf16[16,48,768]{2,1,0:T(8,128)(2,1)S(1)} async-done(((bf16[16,48,768]{2,1,0:T(8,128)(2,1)}), bf16[16,48,768]{2,1,0:T(8,128)(2,1)S(1)}, u32[]{:S(2)}, u32[]{:S(2)}) %all-to-all-start.1) | async-done | bytes 1179680 | tf_op jit(solution)/shard_map/all_to_all | solution.py:49
  53.8 3.7 %all-to-all-start = ((bf16[16,48,768]{2,1,0:T(8,128)(2,1)}), bf16[16,48,768]{2,1,0:T(8,128)(2,1)S(1)}, u32[]{:S(2)}, u32[]{:S(2)}) async-start(bf16[16,48,768]{2,1,0:T(8,128)(2,1)} %bitcast.1), calls=%async_computation | async-start | bytes 2359296 | tf_op jit(solution)/shard_map/all_to_all | solution.py:56
  57.5 0.2 all-reduce.2.cloned.1.call-start
  57.7 10.5 %all-gather.7.cloned.1.call-done = bf16[1,2304,768]{2,1,0:T(8,128)(2,1)} async-done(((bf16[1,144,768]{2,1,0:T(8,128)(2,1)}), bf16[1,2304,768]{2,1,0:T(8,128)(2,1)}) %all-gather.7.cloned.1.call-update) | async-done | bytes 3538960 | tf_op jit(solution)/shard_map/all_gather | solution.py:66
  68.2 7.0 %fusion.9 = f32[768,2304]{1,0:T(8,128)} fusion(bf16[768,768]{1,0:T(8,128)(2,1)S(1)} %bitcast.49, bf16[1,2304,768]{2,1,0:T(8,128)(2,1)} %all-gather.7.cloned.1.call-done), kind=kOutput, calls=%fused_computation.15 | convolution fusion | flops 2717908992 | bytes 11796480 | tf_op jit(solution)/shard_map/dot_general | solution.py:68
  75.2 12.9 %all-to-all-done = bf16[16,48,768]{2,1,0:T(8,128)(2,1)S(1)} async-done(((bf16[16,48,768]{2,1,0:T(8,128)(2,1)}), bf16[16,48,768]{2,1,0:T(8,128)(2,1)S(1)}, u32[]{:S(2)}, u32[]{:S(2)}) %all-to-all-start) | async-done | bytes 1179680 | tf_op jit(solution)/shard_map/all_to_all | solution.py:56
  88.0 8.3 %convolution_convert_fusion = bf16[2304,768]{0,1:T(8,128)(2,1)} fusion(bf16[768,768]{1,0:T(8,128)(2,1)S(1)} %bitcast.51, f32[768,2304]{1,0:T(8,128)} %fusion.9), kind=kOutput, calls=%fused_computation.11 | convolution fusion | flops 2735603712 | bytes 11796480 | tf_op jit(solution)/shard_map/dot_general | solution.py:95
  96.4 27.6 %all-gather.5.cloned.1.call-done = bf16[1,2304,768]{2,1,0:T(8,128)(2,1)} async-done(((bf16[1,144,768]{2,1,0:T(8,128)(2,1)}), bf16[1,2304,768]{2,1,0:T(8,128)(2,1)}) %all-gather.5.cloned.1.call-update) | async-done | bytes 3538960 | tf_op jit(solution)/shard_map/all_gather | solution.py:67
  124.0 8.4 %fusion.6 = bf16[768,2304]{1,0:T(8,128)(2,1)S(1)} fusion(f32[768,2304]{1,0:T(8,128)} %fusion.9, bf16[768,768]{1,0:T(8,128)(2,1)S(1)} %bitcast.52, bf16[1,2304,768]{2,1,0:T(8,128)(2,1)} %all-gather.5.cloned.1.call-done), kind=kOutput, calls=%fused_computation.8 | convolution fusion | flops 2751528960 | bytes 15335424 | tf_op jit(solution)/shard_map/dot_general | solution.py:72
  132.5 1.7 copy-done.3
  134.2 4.7 %convolution_convert_fusion.1 = bf16[2304,768]{0,1:T(8,128)(2,1)} fusion(bf16[768,2304]{1,0:T(8,128)(2,1)S(1)} %fusion.6, bf16[768,768]{1,0:T(8,128)(2,1)S(1)} %bitcast.50), kind=kOutput, calls=%fused_computation.12 | convolution fusion | flops 2719678464 | bytes 8257536 | tf_op jit(solution)/shard_map/dot_general | solution.py:92
  138.9 6.4 %pad_maximum_fusion = bf16[2304,1536]{0,1:T(8,128)(2,1)} fusion(bf16[2304,768]{0,1:T(8,128)(2,1)} %convolution_convert_fusion, bf16[2304,768]{0,1:T(8,128)(2,1)} %convolution_convert_fusion.1), kind=kLoop, calls=%fused_computation.9 | loop fusion | flops 14155776 | bytes 14155776 | tf_op jit(solution)/shard_map/concatenate | solution.py:99
  145.3 7.0 %fusion.16 = bf16[768,768]{1,0:T(8,128)(2,1)} fusion(bf16[768,2304]{1,0:T(8,128)(2,1)} %copy-done.3, bf16[1,2304,768]{2,1,0:T(8,128)(2,1)} %all-gather.7.cloned.1.call-done), kind=kOutput, calls=%fused_computation.23 | convolution fusion | flops 2718498816 | bytes 8257536 | tf_op jit(solution)/shard_map/dot_general | solution.py:76
  152.3 8.1 %all-to-all-start.2 = ((bf16[16,48,768]{2,1,0:T(8,128)(2,1)}), bf16[16,48,768]{2,1,0:T(8,128)(2,1)S(1)}, u32[]{:S(2)}, u32[]{:S(2)}) async-start(bf16[16,48,768]{2,1,0:T(8,128)(2,1)} %bitcast.7), calls=%async_computation.2 | async-start | bytes 2359296 | tf_op jit(solution)/shard_map/all_to_all | solution.py:78
  160.4 30.6 %all-to-all-done.2 = bf16[16,48,768]{2,1,0:T(8,128)(2,1)S(1)} async-done(((bf16[16,48,768]{2,1,0:T(8,128)(2,1)}), bf16[16,48,768]{2,1,0:T(8,128)(2,1)S(1)}, u32[]{:S(2)}, u32[]{:S(2)}) %all-to-all-start.2) | async-done | bytes 1179680 | tf_op jit(solution)/shard_map/all_to_all | solution.py:78
  191.0 1.0 convolution_convert_fusion.3
  192.0 92.4 %all-reduce.2.cloned.1.call-done = bf16[2304,1536]{0,1:T(8,128)(2,1)} async-done(((bf16[2304,1536]{0,1:T(8,128)(2,1)}), bf16[2304,1536]{0,1:T(8,128)(2,1)}) %all-reduce.2.cloned.1.call-update) | async-done | bytes 7077904 | tf_op jit(solution)/shard_map/psum | solution.py:98
  284.4 1.6 dynamic-slice_convert_fusion
  286.0 1.0 copy.33
  287.0 1.0 copy.34
  (18 shorter events, 0.7 us)
Async XLA Ops:
  7.2 4.5 %copy-start = (bf16[128,768]{1,0:T(8,128)(2,1)S(1)}, bf16[128,768]{1,0:T(8,128)(2,1)}, u32[]{:S(2)}) copy-start(bf16[128,768]{1,0:T(8,128)(2,1)} %param.6) | copy-start | bytes 589828
  7.2 16.0 %copy-start.2 = (f32[128,2]{0,1:T(2,128)S(1)}, f32[128,2]{0,1:T(2,128)}, u32[]{:S(2)}) copy-start(f32[128,2]{0,1:T(2,128)} %param.9) | copy-start | bytes 3076
  7.2 16.2 %copy-start.1 = (bf16[128,768]{1,0:T(8,128)(2,1)S(1)}, bf16[128,768]{1,0:T(8,128)(2,1)}, u32[]{:S(2)}) copy-start(bf16[128,768]{1,0:T(8,128)(2,1)} %param.7) | copy-start | bytes 589828
  7.2 61.0 %all-gather.7.cloned.1.call-start = ((), (), s32[]{:S(2)}) async-start(), calls=%async_computation.5 | async-start | bytes 3760128 | tf_op jit(solution)/shard_map/all_gather | solution.py:66
  7.9 116.1 %all-gather.5.cloned.1.call-start = ((), (), s32[]{:S(2)}) async-start(), calls=%async_computation.4 | async-start | bytes 3760128 | tf_op jit(solution)/shard_map/all_gather | solution.py:67
  13.2 40.5 %all-to-all-start.1 = ((bf16[16,48,768]{2,1,0:T(8,128)(2,1)}), bf16[16,48,768]{2,1,0:T(8,128)(2,1)S(1)}, u32[]{:S(2)}, u32[]{:S(2)}) async-start(bf16[16,48,768]{2,1,0:T(8,128)(2,1)} %bitcast.4), calls=%async_computation.1 | async-start | bytes 2359296 | tf_op jit(solution)/shard_map/all_to_all | solution.py:49
  53.8 34.3 %all-to-all-start = ((bf16[16,48,768]{2,1,0:T(8,128)(2,1)}), bf16[16,48,768]{2,1,0:T(8,128)(2,1)S(1)}, u32[]{:S(2)}, u32[]{:S(2)}) async-start(bf16[16,48,768]{2,1,0:T(8,128)(2,1)} %bitcast.1), calls=%async_computation | async-start | bytes 2359296 | tf_op jit(solution)/shard_map/all_to_all | solution.py:56
  57.5 226.9 %all-reduce.2.cloned.1.call-start = ((), (), s32[]{:S(2)}) async-start(), calls=%async_computation.3 | async-start | bytes 14155776 | tf_op jit(solution)/shard_map/psum | solution.py:98
  132.4 1.8 copy-start.3
  152.3 38.6 %all-to-all-start.2 = ((bf16[16,48,768]{2,1,0:T(8,128)(2,1)}), bf16[16,48,768]{2,1,0:T(8,128)(2,1)S(1)}, u32[]{:S(2)}, u32[]{:S(2)}) async-start(bf16[16,48,768]{2,1,0:T(8,128)(2,1)} %bitcast.7), calls=%async_computation.2 | async-start | bytes 2359296 | tf_op jit(solution)/shard_map/all_to_all | solution.py:78
Sparse Core Ops, SparseCore 0:
  10.5 57.6 all-gather.6
  70.6 53.3 all-gather.4
  145.5 138.8 all-reduce.1
where the time goes:
time: 295 us
  waiting for transfers between devices  204 us (69%)
  matrix products  39.5 us (13%)
  starting transfers between devices  22 us (7%)
  between operations  13.8 us (5%)
  other arithmetic  9.72 us (3%)
  local copies, waits for them, and re-layouts  5.32 us (2%)
    psum x1, waiting for transfers between devices, shards(): lax.psum(jnp.concatenate([term_in, term_out], axis=1).astype(jnp.bfloat16...  92.4 us
    all_to_all x1, waiting for transfers between devices, shards(): lax.all_to_all(slot_sum.astype(jnp.bfloat16).reshape(experts, capacity, m...  30.6 us
    all_to_all x1, waiting for transfers between devices, shards(): lax.all_to_all(rows_sent.reshape(experts, capacity, model_width), 'expert...  28.9 us
    all_gather x1, waiting for transfers between devices, shards(): piece_out = lax.all_gather(w_out[0], 'dp', axis=0, tiled=True)  27.6 us
    all_to_all x1, waiting for transfers between devices, shards(): lax.all_to_all(grads_sent.reshape(experts, capacity, model_width), 'exper...  12.9 us
    all_gather x1, waiting for transfers between devices, shards(): piece_in = lax.all_gather(w_in[0], 'dp', axis=0, tiled=True)  10.5 us
    all_to_all x1, starting transfers between devices, shards(): lax.all_to_all(rows_sent.reshape(experts, capacity, model_width), 'expert...  9.98 us
    dot_general x1, matrix products, shards(): lax.dot_general(grads_in, piece_out, (((1,), (1,)), ((), ())), preferred_...  8.45 us
  transfers between devices with their start and end apart: 6, of which 6 were waited for; matrix products, arithmetic and copies ran while one was open for 10% of the time, Pallas kernels for 0%

commit v1 on v0

--- a/solution.py
+++ b/solution.py
@@ -63,7 +63,8 @@
     )
     rows_in = rows_recv.reshape(slot_rows, model_width)
     grads_in = grads_recv.reshape(slot_rows, model_width)
-    piece_in = lax.all_gather(w_in[0], "dp", axis=0, tiled=True)
+    copies = jnp.concatenate([w_in[0]] * lax.axis_size("dp"), axis=0)
+    piece_in = lax.all_to_all(copies, "dp", 0, 0, tiled=True)
     piece_out = lax.all_gather(w_out[0], "dp", axis=0, tiled=True)
     pre = lax.dot_general(
         rows_in, piece_in, (((1,), (1,)), ((), ())), preferred_element_type=jnp.float32

time: 295 us -> 331 us (1.12)
  waiting for transfers between devices: 204 us -> 227 us
  local copies, waits for them, and re-layouts: 5.32 us -> 16.6 us
  starting transfers between devices: 22 us -> 25.4 us
    all_to_all x0 -> x1, waiting for transfers between devices: none -> 62.5 us  [shards(): piece_in = lax.all_to_all(copies, 'dp', 0, 0, tiled=True)]
    all_gather x1, waiting for transfers between devices: 27.6 us -> 0.01 us  [shards(): piece_out = lax.all_gather(w_out[0], 'dp', axis=0, tiled=True)]
    unnamed x11 -> x30, local copies, waits for them, and re-layouts: 4.55 us -> 15.2 us
    all_gather x1 -> x0, waiting for transfers between devices: 10.5 us -> none  [shards(): piece_in = lax.all_gather(w_in[0], 'dp', axis=0, tiled=True)]
    all_to_all x1, waiting for transfers between devices: 12.9 us -> 23.3 us  [shards(): lax.all_to_all(grads_sent.reshape(experts, capacity, model_width), 'exper...]
    all_to_all x1, waiting for transfers between devices: 28.9 us -> 18.6 us  [shards(): lax.all_to_all(rows_sent.reshape(experts, capacity, model_width), 'expert...]
    all_to_all x0 -> x1, starting transfers between devices: none -> 6.93 us  [shards(): piece_in = lax.all_to_all(copies, 'dp', 0, 0, tiled=True)]
    all_to_all x1, starting transfers between devices: 8.06 us -> 3.7 us  [shards(): lax.all_to_all(slot_sum.astype(jnp.bfloat16).reshape(experts, capacity, m...]
  transfers between devices with their start and end apart: 6 -> 6, of which waited for: 6 -> 5; matrix products, arithmetic and copies ran while one was open for 10% -> 11% of each run, Pallas kernels for 0% -> 0%
where the time goes in v1:
time: 331 us
  waiting for transfers between devices  227 us (69%)
  matrix products  39.5 us (12%)
  starting transfers between devices  25.4 us (8%)
  local copies, waits for them, and re-layouts  16.6 us (5%)
  between operations  14.2 us (4%)
  other arithmetic  8.63 us (3%)
    psum x1, waiting for transfers between devices, shards(): lax.psum(jnp.concatenate([term_in, term_out], axis=1).astype(jnp.bfloat16...  90.9 us
    all_to_all x1, waiting for transfers between devices, shards(): piece_in = lax.all_to_all(copies, 'dp', 0, 0, tiled=True)  62.5 us
    all_to_all x1, waiting for transfers between devices, shards(): lax.all_to_all(slot_sum.astype(jnp.bfloat16).reshape(experts, capacity, m...  30.6 us
    all_to_all x1, waiting for transfers between devices, shards(): lax.all_to_all(grads_sent.reshape(experts, capacity, model_width), 'exper...  23.3 us
    all_to_all x1, waiting for transfers between devices, shards(): lax.all_to_all(rows_sent.reshape(experts, capacity, model_width), 'expert...  18.6 us
    unnamed x30, local copies, waits for them, and re-layouts  15.2 us
    all_to_all x1, starting transfers between devices, shards(): lax.all_to_all(rows_sent.reshape(experts, capacity, model_width), 'expert...  9.98 us
    dot_general x1, matrix products, shards(): lax.dot_general(grads_in, piece_out, (((1,), (1,)), ((), ())), preferred_...  8.45 us
  transfers between devices with their start and end apart: 6, of which 5 were waited for; matrix products, arithmetic and copies ran while one was open for 11% of the time, Pallas kernels for 0%

profile of v1, /device:TPU:1, one launch (start us, length us, event | category | flops | bytes accessed | tf_op | source)
XLA Modules:
  0.0 330.9 jit_solution(1747832136231371478)
XLA Ops:
  7.2 0.8 copy.29
  9.4 0.7 multiply_add_fusion.1
  10.3 1.5 convolution_convert_fusion.3
  11.7 10.0 %all-to-all-start.1 = ((bf16[16,48,768]{2,1,0:T(8,128)(2,1)}), bf16[16,48,768]{2,1,0:T(8,128)(2,1)S(1)}, u32[]{:S(2)}, u32[]{:S(2)}) async-start(bf16[16,48,768]{2,1,0:T(8,128)(2,1)} %bitcast.4), calls=%async_computation.1 | async-start | bytes 2359296 | tf_op jit(solution)/shard_map/all_to_all | solution.py:49
  23.8 0.7 bitcast_dynamic-update-slice_fusion.12
  24.6 0.7 bitcast_dynamic-update-slice_fusion.11
  25.3 0.7 bitcast_dynamic-update-slice_fusion.10
  29.5 0.7 bitcast_dynamic-update-slice_fusion.4
  30.2 0.7 bitcast_dynamic-update-slice_fusion.3
  30.9 0.7 bitcast_dynamic-update-slice_fusion.2
  31.6 0.7 bitcast_dynamic-update-slice_fusion.1
  32.3 0.7 bitcast_dynamic-update-slice_fusion
  33.7 18.6 %all-to-all-done.1 = bf16[16,48,768]{2,1,0:T(8,128)(2,1)S(1)} async-done(((bf16[16,48,768]{2,1,0:T(8,128)(2,1)}), bf16[16,48,768]{2,1,0:T(8,128)(2,1)S(1)}, u32[]{:S(2)}, u32[]{:S(2)}) %all-to-all-start.1) | async-done | bytes 1179680 | tf_op jit(solution)/shard_map/all_to_all | solution.py:49
  52.3 6.9 %all-to-all-start.2 = ((bf16[16,144,768]{2,1,0:T(8,128)(2,1)}), bf16[16,144,768]{2,1,0:T(8,128)(2,1)}, u32[]{:S(2)}, u32[]{:S(2)}) async-start(bf16[16,144,768]{2,1,0:T(8,128)(2,1)} %bitcast.7), calls=%async_computation.2 | async-start | bytes 7077888 | tf_op jit(solution)/shard_map/all_to_all | solution.py:67
  59.4 1.5 multiply_convert_fusion.2
  61.0 62.5 %all-to-all-done.2 = bf16[16,144,768]{2,1,0:T(8,128)(2,1)} async-done(((bf16[16,144,768]{2,1,0:T(8,128)(2,1)}), bf16[16,144,768]{2,1,0:T(8,128)(2,1)}, u32[]{:S(2)}, u32[]{:S(2)}) %all-to-all-start.2) | async-done | bytes 3538976 | tf_op jit(solution)/shard_map/all_to_all | solution.py:67
  123.4 4.6 %all-to-all-start = ((bf16[16,48,768]{2,1,0:T(8,128)(2,1)}), bf16[16,48,768]{2,1,0:T(8,128)(2,1)S(1)}, u32[]{:S(2)}, u32[]{:S(2)}) async-start(bf16[16,48,768]{2,1,0:T(8,128)(2,1)} %bitcast.1), calls=%async_computation | async-start | bytes 2359296 | tf_op jit(solution)/shard_map/all_to_all | solution.py:56
  128.2 7.0 %fusion.23 = f32[768,2304]{1,0:T(8,128)} fusion(bf16[768,768]{1,0:T(8,128)(2,1)S(1)} %bitcast.63, bf16[2304,768]{1,0:T(8,128)(2,1)} %bitcast.8), kind=kOutput, calls=%fused_computation.61 | convolution fusion | flops 2717908992 | bytes 11796480 | tf_op jit(solution)/shard_map/dot_general | solution.py:69
  135.2 23.3 %all-to-all-done = bf16[16,48,768]{2,1,0:T(8,128)(2,1)S(1)} async-done(((bf16[16,48,768]{2,1,0:T(8,128)(2,1)}), bf16[16,48,768]{2,1,0:T(8,128)(2,1)S(1)}, u32[]{:S(2)}, u32[]{:S(2)}) %all-to-all-start) | async-done | bytes 1179680 | tf_op jit(solution)/shard_map/all_to_all | solution.py:56
  158.6 8.3 %convolution_convert_fusion = bf16[2304,768]{0,1:T(8,128)(2,1)} fusion(bf16[768,768]{1,0:T(8,128)(2,1)S(1)} %bitcast.65, f32[768,2304]{1,0:T(8,128)} %fusion.23), kind=kOutput, calls=%fused_computation.11 | convolution fusion | flops 2735603712 | bytes 11796480 | tf_op jit(solution)/shard_map/dot_general | solution.py:96
  166.9 8.4 %fusion.6 = bf16[768,2304]{1,0:T(8,128)(2,1)S(1)} fusion(f32[768,2304]{1,0:T(8,128)} %fusion.23, bf16[768,768]{1,0:T(8,128)(2,1)S(1)} %bitcast.66, bf16[1,2304,768]{2,1,0:T(8,128)(2,1)} %all-gather.3.cloned.1.call-done), kind=kOutput, calls=%fused_computation.8 | convolution fusion | flops 2751528960 | bytes 15335424 | tf_op jit(solution)/shard_map/dot_general | solution.py:73
  175.4 1.8 copy-done.5
  177.1 4.7 %convolution_convert_fusion.1 = bf16[2304,768]{0,1:T(8,128)(2,1)} fusion(bf16[768,2304]{1,0:T(8,128)(2,1)S(1)} %fusion.6, bf16[768,768]{1,0:T(8,128)(2,1)S(1)} %bitcast.64), kind=kOutput, calls=%fused_computation.12 | convolution fusion | flops 2719678464 | bytes 8257536 | tf_op jit(solution)/shard_map/dot_general | solution.py:93
  181.8 5.4 %pad_maximum_fusion = bf16[2304,1536]{0,1:T(8,128)(2,1)} fusion(bf16[2304,768]{0,1:T(8,128)(2,1)S(1)} %copy-done.2, bf16[2304,768]{0,1:T(8,128)(2,1)} %convolution_convert_fusion.1), kind=kLoop, calls=%fused_computation.9 | loop fusion | flops 14155776 | bytes 14155776 | tf_op jit(solution)/shard_map/concatenate | solution.py:100
  187.2 7.0 %convolution_convert_fusion.2 = bf16[768,768]{1,0:T(8,128)(2,1)} fusion(bf16[768,2304]{1,0:T(8,128)(2,1)} %copy-done.5, bf16[2304,768]{1,0:T(8,128)(2,1)} %bitcast.8), kind=kOutput, calls=%fused_computation.19 | convolution fusion | flops 2718498816 | bytes 8257536 | tf_op jit(solution)/shard_map/dot_general | solution.py:77
  194.2 3.7 %all-to-all-start.3 = ((bf16[16,48,768]{2,1,0:T(8,128)(2,1)}), bf16[16,48,768]{2,1,0:T(8,128)(2,1)S(1)}, u32[]{:S(2)}, u32[]{:S(2)}) async-start(bf16[16,48,768]{2,1,0:T(8,128)(2,1)} %bitcast.9), calls=%async_computation.3 | async-start | bytes 2359296 | tf_op jit(solution)/shard_map/all_to_all | solution.py:79
  197.9 30.6 %all-to-all-done.3 = bf16[16,48,768]{2,1,0:T(8,128)(2,1)S(1)} async-done(((bf16[16,48,768]{2,1,0:T(8,128)(2,1)}), bf16[16,48,768]{2,1,0:T(8,128)(2,1)S(1)}, u32[]{:S(2)}, u32[]{:S(2)}) %all-to-all-start.3) | async-done | bytes 1179680 | tf_op jit(solution)/shard_map/all_to_all | solution.py:79
  228.5 1.0 convolution_convert_fusion.4
  229.5 90.9 %all-reduce.2.cloned.1.call-done = bf16[2304,1536]{0,1:T(8,128)(2,1)} async-done(((bf16[2304,1536]{0,1:T(8,128)(2,1)}), bf16[2304,1536]{0,1:T(8,128)(2,1)}) %all-reduce.2.cloned.1.call-update) | async-done | bytes 7077904 | tf_op jit(solution)/shard_map/psum | solution.py:99
  320.4 1.6 dynamic-slice_convert_fusion
  322.1 1.0 copy.33
  323.1 1.0 copy.34
  (37 shorter events, 8.3 us)
Async XLA Ops:
  7.2 3.1 copy-start
  7.2 15.3 %copy-start.1 = (bf16[1,144,768]{2,1,0:T(8,128)(2,1)S(1)}, bf16[1,144,768]{2,1,0:T(8,128)(2,1)}, u32[]{:S(2)}) copy-start(bf16[1,144,768]{2,1,0:T(8,128)(2,1)} %param.10) | copy-start | bytes 663556
  11.7 40.5 %all-to-all-start.1 = ((bf16[16,48,768]{2,1,0:T(8,128)(2,1)}), bf16[16,48,768]{2,1,0:T(8,128)(2,1)S(1)}, u32[]{:S(2)}, u32[]{:S(2)}) async-start(bf16[16,48,768]{2,1,0:T(8,128)(2,1)} %bitcast.4), calls=%async_computation.1 | async-start | bytes 2359296 | tf_op jit(solution)/shard_map/all_to_all | solution.py:49
  21.7 145.2 %all-gather.3.cloned.1.call-start = ((), (), s32[]{:S(2)}) async-start(), calls=%async_computation.5 | async-start | bytes 3760128 | tf_op jit(solution)/shard_map/all_gather | solution.py:68
  52.3 6.9 %copy-start.4 = (f32[128,2]{0,1:T(2,128)S(1)}, f32[128,2]{0,1:T(2,128)}, u32[]{:S(2)}) copy-start(f32[128,2]{0,1:T(2,128)} %param.9) | copy-start | bytes 3076
  52.3 7.1 %copy-start.3 = (bf16[128,768]{1,0:T(8,128)(2,1)S(1)}, bf16[128,768]{1,0:T(8,128)(2,1)}, u32[]{:S(2)}) copy-start(bf16[128,768]{1,0:T(8,128)(2,1)} %param.7) | copy-start | bytes 589828
  52.3 71.1 %all-to-all-start.2 = ((bf16[16,144,768]{2,1,0:T(8,128)(2,1)}), bf16[16,144,768]{2,1,0:T(8,128)(2,1)}, u32[]{:S(2)}, u32[]{:S(2)}) async-start(bf16[16,144,768]{2,1,0:T(8,128)(2,1)} %bitcast.7), calls=%async_computation.2 | async-start | bytes 7077888 | tf_op jit(solution)/shard_map/all_to_all | solution.py:67
  123.4 35.1 %all-to-all-start = ((bf16[16,48,768]{2,1,0:T(8,128)(2,1)}), bf16[16,48,768]{2,1,0:T(8,128)(2,1)S(1)}, u32[]{:S(2)}, u32[]{:S(2)}) async-start(bf16[16,48,768]{2,1,0:T(8,128)(2,1)} %bitcast.1), calls=%async_computation | async-start | bytes 2359296 | tf_op jit(solution)/shard_map/all_to_all | solution.py:56
  128.0 192.4 %all-reduce.2.cloned.1.call-start = ((), (), s32[]{:S(2)}) async-start(), calls=%async_computation.4 | async-start | bytes 14155776 | tf_op jit(solution)/shard_map/psum | solution.py:99
  175.4 1.8 copy-start.5
  177.1 4.7 %copy-start.2 = (bf16[2304,768]{0,1:T(8,128)(2,1)S(1)}, bf16[2304,768]{0,1:T(8,128)(2,1)}, u32[]{:S(2)}) copy-start(bf16[2304,768]{0,1:T(8,128)(2,1)} %convolution_convert_fusion) | copy-start | bytes 10616836
  194.2 34.3 %all-to-all-start.3 = ((bf16[16,48,768]{2,1,0:T(8,128)(2,1)}), bf16[16,48,768]{2,1,0:T(8,128)(2,1)S(1)}, u32[]{:S(2)}, u32[]{:S(2)}) async-start(bf16[16,48,768]{2,1,0:T(8,128)(2,1)} %bitcast.9), calls=%async_computation.3 | async-start | bytes 2359296 | tf_op jit(solution)/shard_map/all_to_all | solution.py:79
Sparse Core Ops, SparseCore 0:
  25.0 90.6 all-gather.2
  187.3 133.0 all-reduce.1
